TPU v7x, 128 devices: a whole 4x4x4 slice. The times are simulated.
128 devices in a mesh: seq: 64 (over z, x, y_lo, core), chan: 2 (over y_hi).
Axes of the slice: x: 4, y: 4 (y_hi: 2, y_lo: 2; y = y_hi * 2 + y_lo), z: 4, core: 2. Of those that a mesh axis runs over, the one named last changes fastest.
Arguments:
- signal: bfloat16 [2, 32768, 128], P('chan', 'seq'), may hold values from -6 to 6
- cotangent: bfloat16 [2, 32768, 128], P('chan', 'seq'), may hold values from -6 to 6
- band_freq: int32 [16], replicated, may hold values from 1 to 8191
- w_embed: float32 [32, 64], replicated, may hold values from -2 to 2
- b_embed: float32 [64], replicated, may hold values from -3.140625 to 3.140625
- w_out: float32 [64, 128], P(None, 'chan'), may hold values from -0.75 to 0.75
- decay: float32 [128], P('chan'), may hold values from 0.25 to 16, as said below
Outputs:
- conv_out: bfloat16 [2, 32768, 128], P('chan', 'seq')
- d_signal: bfloat16 [2, 32768, 128], P('chan', 'seq')
- grad_embed: float32 [32, 64], replicated
- grad_bias: float32 [64], replicated
- grad_out: float32 [64, 128], P(None, 'chan')
Inputs may be any that keep to these rules, and one draw needn't show every extreme that they name: decay rates are positive.
All inputs are finite; a program needn't handle non-finite values.
Results may differ from a plain program's by a relative error of at most 0.007.
Values may be sent and summed in bfloat16 or wider, within the bound.
No kernel may reach another device: no remote copies, remote signals or barrier semaphores. Data moves between devices by JAX's collectives and lax.ppermute only.
A program may use at most 192 MiB of HBM per device.

v0:
```python
import math
import jax
import jax.numpy as jnp
from jax import lax
from jax.sharding import PartitionSpec as P

exact_mode = lax.Precision.HIGHEST


def mat_dot(lhs_mat, rhs_mat):
    return jnp.dot(lhs_mat, rhs_mat, preferred_element_type=jnp.float32, precision=exact_mode)


def side_dot(table, values):
    return jnp.einsum(
        "db,cbm->cdm", table, values, preferred_element_type=jnp.float32, precision=exact_mode
    )


def inner_dot(table, values):
    return jnp.einsum(
        "eb,cdbh->cdeh", table, values, preferred_element_type=jnp.float32, precision=exact_mode
    )


def band_phase(band_freq, places, seq_total):
    upper_part = places // 1024
    lower_part = places % 1024
    partial_turn = upper_part[:, None] * band_freq[None, :] % seq_total
    wrapped = (partial_turn * 1024 + lower_part[:, None] * band_freq[None, :]) % seq_total
    return wrapped.astype(jnp.float32) * (2.0 * math.pi / seq_total)


def filter_parts(places, band_freq, w_embed, b_embed, w_out, decay, seq_total):
    phases = band_phase(band_freq, places, seq_total)
    features = jnp.concatenate([jnp.cos(phases), jnp.sin(phases)], axis=1)
    preact = mat_dot(features, w_embed) + b_embed[None, :]
    hidden = jnp.sin(preact)
    fraction = places.astype(jnp.float32) / seq_total
    envelope = (
        jnp.exp(-decay[None, :] * fraction[:, None]) * jnp.sqrt((1.0 + decay) / seq_total)[None, :]
    )
    taps = mat_dot(hidden, w_out) * envelope
    return (features, preact, hidden, taps, envelope)


def angle_table(rows_idx, cols_idx, modulus):
    wrapped = rows_idx[:, None] * cols_idx[None, :] % modulus
    angles = wrapped.astype(jnp.float32) * (2.0 * math.pi / modulus)
    return (jnp.cos(angles), jnp.sin(angles))


def local(signal, cotangent, band_freq, w_embed, b_embed, w_out, decay):
    devices = lax.axis_size("seq")
    rank_seq = lax.axis_index("seq")
    seg_len = signal.shape[1] * 2
    channels = signal.shape[2] // 2
    block_w = seg_len // devices
    rows_all = 2 * devices
    seq_total = seg_len * devices
    fft_size = 2 * seq_total
    inv_scale = 1.0 / fft_size
    radix_one = max(
        (divisor for divisor in range(1, math.isqrt(seg_len) + 1) if seg_len % divisor == 0)
    )
    radix_two = seg_len // radix_one
    row_ids = jnp.arange(rows_all, dtype=jnp.int32)
    src_ids = jnp.arange(devices, dtype=jnp.int32)
    col_glob = rank_seq * block_w + jnp.arange(block_w, dtype=jnp.int32)
    seg_ids = jnp.arange(seg_len, dtype=jnp.int32)
    one_ids = jnp.arange(radix_one, dtype=jnp.int32)
    two_ids = jnp.arange(radix_two, dtype=jnp.int32)
    pair_ids = lax.dynamic_slice_in_dim(row_ids, 2 * rank_seq, 2)
    outer_cos, outer_sin = angle_table(row_ids, src_ids, rows_all)
    entry_cos, entry_sin = angle_table(row_ids, col_glob, fft_size)
    first_cos, first_sin = angle_table(one_ids, one_ids, radix_one)
    second_cos, second_sin = angle_table(two_ids, two_ids, radix_two)
    inner_cos, inner_sin = angle_table(one_ids, two_ids, seg_len)
    exit_cos, exit_sin = angle_table(pair_ids, seg_ids, fft_size)
    inner_c = inner_cos[None, :, :, None]
    inner_s = inner_sin[None, :, :, None]

    def twist_stack(real_a, imag_a):
        real_a = real_a.reshape(rows_all, block_w, channels)
        imag_a = imag_a.reshape(rows_all, block_w, channels)
        twist_c = entry_cos[:, :, None]
        twist_s = entry_sin[:, :, None]
        real_b = real_a * twist_c + imag_a * twist_s
        imag_b = imag_a * twist_c - real_a * twist_s
        return jnp.stack([real_b, imag_b]).reshape(2, rows_all, block_w * channels)

    def column_pass(cols_data):
        return twist_stack(mat_dot(outer_cos, cols_data), -mat_dot(outer_sin, cols_data))

    def local_forward(stacked):
        grid = stacked.reshape(2, 2, radix_one, radix_two * channels)
        part_r = side_dot(first_cos, grid[0]) + side_dot(first_sin, grid[1])
        part_i = side_dot(first_cos, grid[1]) - side_dot(first_sin, grid[0])
        part_r = part_r.reshape(2, radix_one, radix_two, channels)
        part_i = part_i.reshape(2, radix_one, radix_two, channels)
        turn_r = part_r * inner_c + part_i * inner_s
        turn_i = part_i * inner_c - part_r * inner_s
        spec_r = inner_dot(second_cos, turn_r) + inner_dot(second_sin, turn_i)
        spec_i = inner_dot(second_cos, turn_i) - inner_dot(second_sin, turn_r)
        return (spec_r, spec_i)

    def local_inverse(spec_r, spec_i):
        back_r = inner_dot(second_cos, spec_r) - inner_dot(second_sin, spec_i)
        back_i = inner_dot(second_cos, spec_i) + inner_dot(second_sin, spec_r)
        turn_r = (back_r * inner_c - back_i * inner_s).reshape(2, radix_one, radix_two * channels)
        turn_i = (back_r * inner_s + back_i * inner_c).reshape(2, radix_one, radix_two * channels)
        time_r = (side_dot(first_cos, turn_r) - side_dot(first_sin, turn_i)).reshape(
            2, seg_len, channels
        )
        time_i = (side_dot(first_cos, turn_i) + side_dot(first_sin, turn_r)).reshape(
            2, seg_len, channels
        )
        twist_c = exit_cos[:, :, None]
        twist_s = exit_sin[:, :, None]
        final_r = time_r * twist_c - time_i * twist_s
        final_i = time_r * twist_s + time_i * twist_c
        return jnp.stack([final_r, final_i]).reshape(2, 2, seg_len * channels)

    def real_rows(gathered):
        return mat_dot(outer_cos.T, gathered[0]) - mat_dot(outer_sin.T, gathered[1])

    sig_cols, cot_cols = (
        lax.all_to_all(
            signal.reshape(devices, block_w * channels),
            "seq",
            split_axis=0,
            concat_axis=0,
            tiled=True,
        ),
        lax.all_to_all(
            cotangent.reshape(devices, block_w * channels),
            "seq",
            split_axis=0,
            concat_axis=0,
            tiled=True,
        ),
    )
    places = rank_seq * seg_len + seg_ids
    features, preact, hidden, taps, envelope = filter_parts(
        places, band_freq, w_embed, b_embed, w_out, decay, seq_total
    )
    tap_cols = lax.all_to_all(
        taps.reshape(devices, block_w * channels), "seq", split_axis=0, concat_axis=0, tiled=True
    )
    spec_sig, spec_cot, spec_tap = (
        lax.all_to_all(
            column_pass(sig_cols.astype(jnp.float32)),
            "seq",
            split_axis=1,
            concat_axis=2,
            tiled=True,
        ),
        lax.all_to_all(
            column_pass(cot_cols.astype(jnp.float32)),
            "seq",
            split_axis=1,
            concat_axis=2,
            tiled=True,
        ),
        lax.all_to_all(column_pass(tap_cols), "seq", split_axis=1, concat_axis=2, tiled=True),
    )
    sig_r, sig_i = local_forward(spec_sig)
    cot_r, cot_i = local_forward(spec_cot)
    tap_r, tap_i = local_forward(spec_tap)
    prod_r = sig_r * tap_r - sig_i * tap_i
    prod_i = sig_r * tap_i + sig_i * tap_r
    grad_r = cot_r * tap_r + cot_i * tap_i
    grad_i = cot_i * tap_r - cot_r * tap_i
    corr_r = cot_r * sig_r + cot_i * sig_i
    corr_i = cot_i * sig_r - cot_r * sig_i
    prod_back, grad_back, corr_back = (
        lax.all_to_all(
            local_inverse(prod_r, prod_i), "seq", split_axis=2, concat_axis=1, tiled=True
        ),
        lax.all_to_all(
            local_inverse(grad_r, grad_i), "seq", split_axis=2, concat_axis=1, tiled=True
        ),
        lax.all_to_all(
            local_inverse(corr_r, corr_i), "seq", split_axis=2, concat_axis=1, tiled=True
        ),
    )
    out_cols = real_rows(prod_back)
    dsig_cols = real_rows(grad_back)
    dtap_cols = real_rows(corr_back) * inv_scale
    out_rows, dsig_rows = (
        lax.all_to_all(
            (out_cols * inv_scale).astype(jnp.bfloat16),
            "seq",
            split_axis=0,
            concat_axis=0,
            tiled=True,
        ),
        lax.all_to_all(
            (dsig_cols * inv_scale).astype(jnp.bfloat16),
            "seq",
            split_axis=0,
            concat_axis=0,
            tiled=True,
        ),
    )
    conv_out = out_rows.reshape(1, seg_len // 2, 2 * channels)
    d_signal = dsig_rows.reshape(1, seg_len // 2, 2 * channels)
    d_taps = (
        lax.all_to_all(
            dtap_cols.astype(jnp.bfloat16), "seq", split_axis=0, concat_axis=0, tiled=True
        )
        .astype(dtap_cols.dtype)
        .reshape(seg_len, channels)
    )
    d_raw = d_taps * envelope
    d_preact = mat_dot(d_raw, w_out.T) * jnp.cos(preact)
    out_part = mat_dot(hidden.T, d_raw)
    embed_part = mat_dot(features.T, d_preact)
    bias_part = jnp.sum(d_preact, axis=0)
    out_sum, embed_sum, bias_sum = lax.psum((out_part, embed_part, bias_part), "seq")
    embed_all, bias_all = lax.psum((embed_sum, bias_sum), "chan")
    norm_scale = 1.0 / math.sqrt(seq_total)
    return (conv_out, d_signal, embed_all * norm_scale, bias_all * norm_scale, out_sum * norm_scale)


def solution(mesh):
    return jax.shard_map(
        local,
        mesh=mesh,
        in_specs=(
            P("chan", "seq", None),
            P("chan", "seq", None),
            P(),
            P(),
            P(),
            P(None, "chan"),
            P("chan"),
        ),
        out_specs=(P("chan", "seq", None), P("chan", "seq", None), P(), P(), P(None, "chan")),
        check_vma=False,
    )
```

profile of v0, /device:TPU:0, one launch (start us, length us, event | category | flops | bytes accessed | tf_op | source)
XLA Modules:
  0.0 1673.4 jit_solution(10459679201133411678)
XLA Ops:
  4.5 9.9 all-to-all-start
  24.7 8.8 all-to-all-start.6
  34.2 7.9 all-to-all-done.6
  42.1 5.1 all-to-all-start.2
  49.2 7.9 all-to-all-done.2
  67.4 4.7 all-to-all-start.3
  84.9 5.3 all-to-all-done.3
  90.2 4.7 all-to-all-start.1
  101.8 11.2 all-to-all-done.1
  113.0 5.7 all-to-all-start.7
  228.6 58.0 %copy.88 = f32[2,2,65536]{1,0,2:T(2,128)} copy(f32[2,2,65536]{2,1,0:T(2,128)S(1)} %pad_maximum_fusion.2) | data formatting | bytes 2097152 | tf_op jit(solution)/shard_map/stack | solution.py:122
  286.6 96.8 %reshape.642 = f32[64,1,4096]{2,1,0:T(1,128)} reshape(f32[65536,2,2]{2,1,0:T(2,128)} %bitcast.255) | data formatting | bytes 2097152
  383.4 8.7 all-to-all-start.4
  392.7 58.0 %copy.98 = f32[2,2,65536]{1,0,2:T(2,128)} copy(f32[2,2,65536]{2,1,0:T(2,128)S(1)} %pad_maximum_fusion.4) | data formatting | bytes 2097152 | tf_op jit(solution)/shard_map/stack | solution.py:122
  450.7 96.8 %reshape.648 = f32[64,1,4096]{2,1,0:T(1,128)} reshape(f32[65536,2,2]{2,1,0:T(2,128)} %bitcast.257) | data formatting | bytes 2097152
  547.5 8.8 all-to-all-start.8
  558.0 58.0 %copy.101 = f32[2,2,65536]{1,0,2:T(2,128)} copy(f32[2,2,65536]{2,1,0:T(2,128)S(1)} %pad_maximum_fusion.5) | data formatting | bytes 2097152 | tf_op jit(solution)/shard_map/stack | solution.py:122
  616.0 96.8 %reshape.652 = f32[64,1,4096]{2,1,0:T(1,128)} reshape(f32[65536,2,2]{2,1,0:T(2,128)} %bitcast.259) | data formatting | bytes 2097152
  716.5 129.2 %reshape.643 = f32[65536,2,2]{2,1,0:T(2,128)} reshape(f32[64,4096]{1,0:T(8,128)S(1)} %reduce.6) | data formatting | bytes 2097152
  845.8 71.0 %copy.89 = f32[2,2,64,1024]{3,1,2,0:T(2,128)S(1)} copy(f32[2,2,64,1024]{1,0,3,2:T(2,128)} %bitcast.35) | data formatting | bytes 2097152 | tf_op jit(solution)/shard_map/all_to_all | solution.py:177
  917.6 9.1 all-to-all-start.10
  932.4 129.0 %reshape.649 = f32[65536,2,2]{2,1,0:T(2,128)} reshape(f32[64,4096]{1,0:T(8,128)S(1)} %reduce.8) | data formatting | bytes 2097152
  1061.4 71.0 %copy.99 = f32[2,2,64,1024]{3,1,2,0:T(2,128)S(1)} copy(f32[2,2,64,1024]{1,0,3,2:T(2,128)} %bitcast.54) | data formatting | bytes 2097152 | tf_op jit(solution)/shard_map/all_to_all | solution.py:180
  1135.7 9.4 all-to-all-start.5
  1148.4 129.0 %reshape.653 = f32[65536,2,2]{2,1,0:T(2,128)} reshape(f32[64,4096]{1,0:T(8,128)S(1)} %reduce.10) | data formatting | bytes 2097152
  1277.5 71.0 %copy.102 = f32[2,2,64,1024]{3,1,2,0:T(2,128)S(1)} copy(f32[2,2,64,1024]{1,0,3,2:T(2,128)} %bitcast.63) | data formatting | bytes 2097152 | tf_op jit(solution)/shard_map/all_to_all | solution.py:183
  1349.8 9.1 all-to-all-start.9
  1360.9 6.4 all-to-all-done.9
  1367.4 4.6 all-to-all-start.11
  1375.1 5.4 all-to-all-done.11
  1383.9 276.3 %all-reduce = (f32[32,64]{1,0:T(8,128)S(1)}, f32[64]{0:T(128)S(1)}, f32[64,64]{1,0:T(8,128)S(1)}) all-reduce(f32[32,64]{1,0:T(8,128)S(1)} %fusion.61, f32[64]{0:T(128)S(1)} %get-tuple-element.72, f32[64,64]{1,0:T(8,128)S(1)} %fusion.48), channel_id=1, replica_groups=mesh['seq'=64,'chan'=2] {'seq'}, use_global_device_ids=true, to_apply=%region_0.1 | all-reduce | flops 6208 | bytes 49664 | tf_op jit(solution)/shard_map/psum | solution.py:220
  1660.2 11.2 all-reduce.1
  (216 shorter events, 186.5 us)
Async XLA Ops:
  0.6 22.3 %copy-start = (f32[64,64]{1,0:T(8,128)S(1)}, f32[64,64]{1,0:T(8,128)}, u32[]{:S(2)}) copy-start(f32[64,64]{1,0:T(8,128)} %param.12) | copy-start | bytes 49156
  4.5 20.2 %all-to-all-start = ((bf16[64,2,512]{2,1,0:T(2,128)(2,1)}), bf16[64,2,512]{2,1,0:T(2,128)(2,1)S(1)}, u32[]{:S(2)}, u32[]{:S(2)}) async-start(bf16[64,2,512]{2,1,0:T(2,128)(2,1)} %reshape.640), calls=%async_computation | async-start | bytes 262144 | tf_op jit(solution)/shard_map/all_to_all | solution.py:128
  14.4 7.8 copy-start.12
  15.1 7.1 copy-start.14
  15.1 7.1 copy-start.16
  19.5 2.7 copy-start.8
  19.5 2.7 copy-start.10
  22.2 0.7 copy-start.3
  24.7 17.4 %all-to-all-start.6 = ((bf16[64,2,512]{2,1,0:T(2,128)(2,1)}), bf16[64,2,512]{2,1,0:T(2,128)(2,1)S(1)}, u32[]{:S(2)}, u32[]{:S(2)}) async-start(bf16[64,2,512]{2,1,0:T(2,128)(2,1)} %reshape.646), calls=%async_computation.6 | async-start | bytes 262144 | tf_op jit(solution)/shard_map/all_to_all | solution.py:135
  42.1 15.0 all-to-all-start.2
  67.4 22.7 %all-to-all-start.3 = ((f32[2,128,1024]{2,0,1:T(2,128)}), f32[2,128,1024]{2,0,1:T(2,128)S(1)}, u32[]{:S(2)}, u32[]{:S(2)}) async-start(f32[2,128,1024]{2,0,1:T(2,128)} %pad_maximum_fusion.1), calls=%async_computation.3 | async-start | bytes 2097152 | tf_op jit(solution)/shard_map/all_to_all | solution.py:165
  90.2 22.8 %all-to-all-start.1 = ((f32[2,128,1024]{2,0,1:T(2,128)}), f32[2,128,1024]{2,0,1:T(2,128)S(1)}, u32[]{:S(2)}, u32[]{:S(2)}) async-start(f32[2,128,1024]{2,0,1:T(2,128)} %pad_maximum_fusion), calls=%async_computation.1 | async-start | bytes 2097152 | tf_op jit(solution)/shard_map/all_to_all | solution.py:151
  113.0 29.0 %all-to-all-start.7 = ((f32[2,128,1024]{2,0,1:T(2,128)}), f32[2,128,1024]{2,0,1:T(2,128)}, u32[]{:S(2)}, u32[]{:S(2)}) async-start(f32[2,128,1024]{2,0,1:T(2,128)} %pad_maximum_fusion.3), calls=%async_computation.7 | async-start | bytes 2097152 | tf_op jit(solution)/shard_map/all_to_all | solution.py:158
  123.7 36.2 %copy-start.1 = (f32[2,32,32,64]{3,2,1,0:T(8,128)}, f32[2,32,32,64]{3,2,1,0:T(8,128)S(1)}, u32[]{:S(2)}) copy-start(f32[2,32,32,64]{3,2,1,0:T(8,128)S(1)} %reshape.610) | copy-start | bytes 1572868
  129.9 32.5 %copy-start.2 = (f32[2,32,32,64]{3,2,1,0:T(8,128)}, f32[2,32,32,64]{3,2,1,0:T(8,128)S(1)}, u32[]{:S(2)}) copy-start(f32[2,32,32,64]{3,2,1,0:T(8,128)S(1)} %reshape.613) | copy-start | bytes 1572868
  228.6 163.6 %copy-start.5 = (f32[1,2,65536]{2,1,0:T(2,128)S(1)}, f32[1,2,65536]{2,1,0:T(2,128)}, u32[]{:S(2)}) copy-start(f32[1,2,65536]{2,1,0:T(2,128)} %get-tuple-element.40) | copy-start | bytes 1572868
  228.6 163.6 %copy-start.6 = (f32[1,2,65536]{2,1,0:T(2,128)S(1)}, f32[1,2,65536]{2,1,0:T(2,128)}, u32[]{:S(2)}) copy-start(f32[1,2,65536]{2,1,0:T(2,128)} %get-tuple-element.41) | copy-start | bytes 1572868
  383.4 164.0 %all-to-all-start.4 = ((f32[64,1,4096]{2,1,0:T(1,128)}), f32[64,1,4096]{2,1,0:T(1,128)S(1)}, u32[]{:S(2)}, u32[]{:S(2)}) async-start(f32[64,1,4096]{2,1,0:T(1,128)} %reshape.642), calls=%async_computation.4 | async-start | bytes 2097152 | tf_op jit(solution)/shard_map/all_to_all | solution.py:177
  547.5 370.1 %all-to-all-start.8 = ((f32[64,1,4096]{2,1,0:T(1,128)}), f32[64,1,4096]{2,1,0:T(1,128)S(1)}, u32[]{:S(2)}, u32[]{:S(2)}) async-start(f32[64,1,4096]{2,1,0:T(1,128)} %reshape.648), calls=%async_computation.8 | async-start | bytes 2097152 | tf_op jit(solution)/shard_map/all_to_all | solution.py:180
  917.6 218.2 %all-to-all-start.10 = ((f32[64,1,4096]{2,1,0:T(1,128)}), f32[64,1,4096]{2,1,0:T(1,128)S(1)}, u32[]{:S(2)}, u32[]{:S(2)}) async-start(f32[64,1,4096]{2,1,0:T(1,128)} %reshape.652), calls=%async_computation.10 | async-start | bytes 2097152 | tf_op jit(solution)/shard_map/all_to_all | solution.py:183
  1135.7 214.1 %all-to-all-start.5 = ((bf16[64,2,512]{2,1,0:T(2,128)(2,1)}), bf16[64,2,512]{2,1,0:T(2,128)(2,1)S(1)}, u32[]{:S(2)}, u32[]{:S(2)}) async-start(bf16[64,2,512]{2,1,0:T(2,128)(2,1)} %reshape.644), calls=%async_computation.5 | async-start | bytes 262144 | tf_op jit(solution)/shard_map/all_to_all | solution.py:191
  1148.4 233.3 %copy-start.4 = (f32[1024,64]{0,1:T(8,128)S(1)}, f32[1024,64]{0,1:T(8,128)}, u32[]{:S(2)}) copy-start(f32[1024,64]{0,1:T(8,128)} %copy-done.3) | copy-start | bytes 786436
  1148.4 233.3 %copy-start.13 = (f32[1024]{0:T(1024)S(1)}, f32[1024]{0:T(1024)}, u32[]{:S(2)}) copy-start(f32[1024]{0:T(1024)} %copy-done.12) | copy-start | bytes 12292
  1148.4 233.3 %copy-start.15 = (f32[64]{0:T(128)S(1)}, f32[64]{0:T(128)}, u32[]{:S(2)}) copy-start(f32[64]{0:T(128)} %copy-done.14) | copy-start | bytes 772
  1148.4 233.3 %copy-start.17 = (f32[64]{0:T(128)S(1)}, f32[64]{0:T(128)}, u32[]{:S(2)}) copy-start(f32[64]{0:T(128)} %copy-done.16) | copy-start | bytes 772
  1148.4 233.8 %copy-start.7 = (f32[1024,64]{0,1:T(8,128)S(1)}, f32[1024,64]{0,1:T(8,128)}, u32[]{:S(2)}) copy-start(f32[1024,64]{0,1:T(8,128)} %get-tuple-element.71) | copy-start | bytes 786436
  1148.4 235.1 %copy-start.9 = (f32[1024,16]{0,1:T(8,128)S(1)}, f32[1024,16]{0,1:T(8,128)}, u32[]{:S(2)}) copy-start(f32[1024,16]{0,1:T(8,128)} %copy-done.8) | copy-start | bytes 196612
  1148.4 235.1 %copy-start.11 = (f32[1024,16]{0,1:T(8,128)S(1)}, f32[1024,16]{0,1:T(8,128)}, u32[]{:S(2)}) copy-start(f32[1024,16]{0,1:T(8,128)} %copy-done.10) | copy-start | bytes 196612
  1349.8 17.5 %all-to-all-start.9 = ((bf16[64,2,512]{2,1,0:T(2,128)(2,1)}), bf16[64,2,512]{2,1,0:T(2,128)(2,1)S(1)}, u32[]{:S(2)}, u32[]{:S(2)}) async-start(bf16[64,2,512]{2,1,0:T(2,128)(2,1)} %reshape.650), calls=%async_computation.9 | async-start | bytes 262144 | tf_op jit(solution)/shard_map/all_to_all | solution.py:198
  1367.4 13.2 all-to-all-start.11
where the time goes:
time: 1690 us; the launch traced here: 1670 us
  local copies, waits for them, and re-layouts  1130 us (67%)
  blocking collectives  288 us (17%)
  matrix products  88.8 us (5%)
  starting transfers between devices  88.6 us (5%)
  waiting for transfers between devices  44.2 us (3%)
  other arithmetic  33.8 us (2%)
    unnamed x52, local copies, waits for them, and re-layouts  683 us
    psum x1, blocking collectives, local(): lax.psum((out_part, embed_part, bias_part), 'seq')  276 us
    another operation x3, local copies, waits for them, and re-layouts, local_inverse(): return jnp.stack([final_r, final_i]).reshape(2, 2, seg_len * channels)  174 us
    all_to_all x2, local copies, waits for them, and re-layouts, local(): lax.all_to_all(local_inverse(prod_r, prod_i), 'seq', split_axis=2, concat...  71.5 us
    all_to_all x1, local copies, waits for them, and re-layouts, local(): lax.all_to_all(local_inverse(corr_r, corr_i), 'seq', split_axis=2, concat...  71 us
    all_to_all x1, local copies, waits for them, and re-layouts, local(): lax.all_to_all(local_inverse(grad_r, grad_i), 'seq', split_axis=2, concat...  71 us
    dot_general x24, matrix products, inner_dot(): jnp.einsum('eb,cdbh->cdeh', table, values, preferred_element_type=jnp.flo...  45 us
  transfers between devices with their start and end apart: 12, of which 6 were waited for; matrix products, arithmetic and copies ran while one was open for 59% of the time, Pallas kernels for 0%

commit v1 on v0

--- a/solution.py
+++ b/solution.py
@@ -5,6 +5,13 @@
 from jax.sharding import PartitionSpec as P
 
 exact_mode = lax.Precision.HIGHEST
+
+
+def trade_parts(x, axis, split, join):
+    size = lax.axis_size(axis)
+    blocks = jnp.stack(jnp.split(x, size, axis=split), axis=0)
+    blocks = lax.all_to_all(blocks, axis, split_axis=0, concat_axis=0)
+    return jnp.concatenate(blocks, axis=join)
 
 
 def mat_dot(lhs_mat, rhs_mat):
@@ -174,9 +181,7 @@
     corr_r = cot_r * sig_r + cot_i * sig_i
     corr_i = cot_i * sig_r - cot_r * sig_i
     prod_back, grad_back, corr_back = (
-        lax.all_to_all(
-            local_inverse(prod_r, prod_i), "seq", split_axis=2, concat_axis=1, tiled=True
-        ),
+        trade_parts(local_inverse(prod_r, prod_i), "seq", 2, 1),
         lax.all_to_all(
             local_inverse(grad_r, grad_i), "seq", split_axis=2, concat_axis=1, tiled=True
         ),

time: 1690 us -> 1370 us (0.81)
  local copies, waits for them, and re-layouts: 1130 us -> 775 us
  other arithmetic: 33.8 us -> 68.9 us
    unnamed x52 -> x50, local copies, waits for them, and re-layouts: 683 us -> 457 us
    all_to_all x2 -> x0, local copies, waits for them, and re-layouts: 71.5 us -> none  [local(): lax.all_to_all(local_inverse(prod_r, prod_i), 'seq', split_axis=2, concat...]
    another operation x3 -> x2, local copies, waits for them, and re-layouts: 174 us -> 116 us  [local_inverse(): return jnp.stack([final_r, final_i]).reshape(2, 2, seg_len * channels)]
    unnamed x0 -> x63, other arithmetic: none -> 38.2 us
    all_to_all x1 -> x2, local copies, waits for them, and re-layouts: 71 us -> 71.5 us  [local(): lax.all_to_all(local_inverse(grad_r, grad_i), 'seq', split_axis=2, concat...]
  transfers between devices with their start and end apart: 12 -> 12, of which waited for: 6 -> 6; matrix products, arithmetic and copies ran while one was open for 59% -> 58% of each run, Pallas kernels for 0% -> 0%
where the time goes in v1:
time: 1370 us; the launch traced here: 1360 us
  local copies, waits for them, and re-layouts  775 us (57%)
  blocking collectives  287 us (21%)
  starting transfers between devices  96.8 us (7%)
  matrix products  88.7 us (6%)
  other arithmetic  68.9 us (5%)
  waiting for transfers between devices  44 us (3%)
    unnamed x50, local copies, waits for them, and re-layouts  457 us
    psum x1, blocking collectives, local(): lax.psum((out_part, embed_part, bias_part), 'seq')  276 us
    another operation x2, local copies, waits for them, and re-layouts, local_inverse(): return jnp.stack([final_r, final_i]).reshape(2, 2, seg_len * channels)  116 us
    all_to_all x2, local copies, waits for them, and re-layouts, local(): lax.all_to_all(local_inverse(grad_r, grad_i), 'seq', split_axis=2, concat...  71.5 us
    all_to_all x1, local copies, waits for them, and re-layouts, local(): lax.all_to_all(local_inverse(corr_r, corr_i), 'seq', split_axis=2, concat...  71 us
    dot_general x24, matrix products, inner_dot(): jnp.einsum('eb,cdbh->cdeh', table, values, preferred_element_type=jnp.flo...  45 us
    unnamed x63, other arithmetic  38.2 us
    dot_general x24, matrix products, side_dot(): jnp.einsum('db,cbm->cdm', table, values, preferred_element_type=jnp.float...  29.2 us
  transfers between devices with their start and end apart: 12, of which 6 were waited for; matrix products, arithmetic and copies ran while one was open for 58% of the time, Pallas kernels for 0%

profile of v1, /device:TPU:0, one launch (start us, length us, event | category | flops | bytes accessed | tf_op | source)
XLA Modules:
  0.0 1363.3 jit_solution(13126591315604744971)
XLA Ops:
  4.5 9.9 all-to-all-start
  24.7 8.8 all-to-all-start.6
  34.2 7.9 all-to-all-done.6
  42.1 4.9 all-to-all-start.2
  49.0 7.9 all-to-all-done.2
  67.2 4.7 all-to-all-start.3
  84.7 5.2 all-to-all-done.3
  89.9 4.7 all-to-all-start.1
  101.6 11.2 all-to-all-done.1
  112.7 14.3 %all-to-all-start.7 = ((f32[2,128,1024]{2,0,1:T(2,128)}), f32[2,128,1024]{2,0,1:T(2,128)}, u32[]{:S(2)}, u32[]{:S(2)}) async-start(f32[2,128,1024]{2,0,1:T(2,128)} %pad_maximum_fusion.2), calls=%async_computation.7 | async-start | bytes 2097152 | tf_op jit(solution)/shard_map/all_to_all | solution.py:165
  146.8 3.5 fusion.41
  150.2 3.8 fusion.548
  184.9 3.6 convolution_add_fusion.10
  232.7 3.7 multiply_subtract_fusion.6
  275.2 8.8 all-to-all-start.4
  284.5 57.8 %copy.93 = f32[2,2,65536]{1,0,2:T(2,128)} copy(f32[2,2,65536]{2,1,0:T(2,128)S(1)} %pad_maximum_fusion.3) | data formatting | bytes 2097152 | tf_op jit(solution)/shard_map/stack | solution.py:129
  342.3 96.8 %reshape.651 = f32[64,1,4096]{2,1,0:T(1,128)} reshape(f32[65536,2,2]{2,1,0:T(2,128)} %bitcast.388) | data formatting | bytes 2097152
  439.0 8.8 all-to-all-start.8
  449.6 57.8 %copy.96 = f32[2,2,65536]{1,0,2:T(2,128)} copy(f32[2,2,65536]{2,1,0:T(2,128)S(1)} %pad_maximum_fusion.4) | data formatting | bytes 2097152 | tf_op jit(solution)/shard_map/stack | solution.py:129
  507.4 96.8 %reshape.655 = f32[64,1,4096]{2,1,0:T(1,128)} reshape(f32[65536,2,2]{2,1,0:T(2,128)} %bitcast.390) | data formatting | bytes 2097152
  606.8 9.0 all-to-all-start.10
  622.1 129.1 %reshape.652 = f32[65536,2,2]{2,1,0:T(2,128)} reshape(f32[64,4096]{1,0:T(8,128)S(1)} %reduce.7) | data formatting | bytes 2097152
  751.3 71.0 %copy.94 = f32[2,2,64,1024]{3,1,2,0:T(2,128)S(1)} copy(f32[2,2,64,1024]{1,0,3,2:T(2,128)} %bitcast.117) | data formatting | bytes 2097152 | tf_op jit(solution)/shard_map/all_to_all | solution.py:185
  825.6 9.2 all-to-all-start.5
  838.1 129.1 %reshape.656 = f32[65536,2,2]{2,1,0:T(2,128)} reshape(f32[64,4096]{1,0:T(8,128)S(1)} %reduce.9) | data formatting | bytes 2097152
  967.2 71.0 %copy.97 = f32[2,2,64,1024]{3,1,2,0:T(2,128)S(1)} copy(f32[2,2,64,1024]{1,0,3,2:T(2,128)} %bitcast.126) | data formatting | bytes 2097152 | tf_op jit(solution)/shard_map/all_to_all | solution.py:188
  1039.6 9.2 all-to-all-start.9
  1050.7 6.3 all-to-all-done.9
  1057.1 4.6 all-to-all-start.11
  1064.8 5.4 all-to-all-done.11
  1073.6 276.3 %all-reduce = (f32[32,64]{1,0:T(8,128)S(1)}, f32[64]{0:T(128)S(1)}, f32[64,64]{1,0:T(8,128)S(1)}) all-reduce(f32[32,64]{1,0:T(8,128)S(1)} %fusion.61, f32[64]{0:T(128)S(1)} %get-tuple-element.72, f32[64,64]{1,0:T(8,128)S(1)} %fusion.48), channel_id=1, replica_groups=mesh['seq'=64,'chan'=2] {'seq'}, use_global_device_ids=true, to_apply=%region_0.1 | all-reduce | flops 6208 | bytes 49664 | tf_op jit(solution)/shard_map/psum | solution.py:225
  1350.0 11.2 all-reduce.1
  (274 shorter events, 208.9 us)
Async XLA Ops:
  0.6 22.3 %copy-start = (f32[64,64]{1,0:T(8,128)S(1)}, f32[64,64]{1,0:T(8,128)}, u32[]{:S(2)}) copy-start(f32[64,64]{1,0:T(8,128)} %param.12) | copy-start | bytes 49156
  4.5 20.2 %all-to-all-start = ((bf16[64,2,512]{2,1,0:T(2,128)(2,1)}), bf16[64,2,512]{2,1,0:T(2,128)(2,1)S(1)}, u32[]{:S(2)}, u32[]{:S(2)}) async-start(bf16[64,2,512]{2,1,0:T(2,128)(2,1)} %reshape.645), calls=%async_computation | async-start | bytes 262144 | tf_op jit(solution)/shard_map/all_to_all | solution.py:135
  14.4 7.8 copy-start.12
  15.1 7.1 copy-start.14
  15.1 7.1 copy-start.16
  19.5 2.7 copy-start.8
  19.5 2.7 copy-start.10
  22.2 0.7 copy-start.3
  24.7 17.4 %all-to-all-start.6 = ((bf16[64,2,512]{2,1,0:T(2,128)(2,1)}), bf16[64,2,512]{2,1,0:T(2,128)(2,1)S(1)}, u32[]{:S(2)}, u32[]{:S(2)}) async-start(bf16[64,2,512]{2,1,0:T(2,128)(2,1)} %reshape.649), calls=%async_computation.6 | async-start | bytes 262144 | tf_op jit(solution)/shard_map/all_to_all | solution.py:142
  42.1 14.8 %all-to-all-start.2 = ((f32[64,1,1024]{2,1,0:T(1,128)}), f32[64,1,1024]{2,1,0:T(1,128)S(1)}, u32[]{:S(2)}, u32[]{:S(2)}) async-start(f32[64,1,1024]{2,1,0:T(1,128)} %all_to_all.132), calls=%async_computation.2 | async-start | bytes 524288 | tf_op jit(solution)/shard_map/all_to_all | solution.py:154
  67.2 22.7 %all-to-all-start.3 = ((f32[2,128,1024]{2,0,1:T(2,128)}), f32[2,128,1024]{2,0,1:T(2,128)S(1)}, u32[]{:S(2)}, u32[]{:S(2)}) async-start(f32[2,128,1024]{2,0,1:T(2,128)} %pad_maximum_fusion.1), calls=%async_computation.3 | async-start | bytes 2097152 | tf_op jit(solution)/shard_map/all_to_all | solution.py:172
  89.9 22.8 %all-to-all-start.1 = ((f32[2,128,1024]{2,0,1:T(2,128)}), f32[2,128,1024]{2,0,1:T(2,128)S(1)}, u32[]{:S(2)}, u32[]{:S(2)}) async-start(f32[2,128,1024]{2,0,1:T(2,128)} %pad_maximum_fusion), calls=%async_computation.1 | async-start | bytes 2097152 | tf_op jit(solution)/shard_map/all_to_all | solution.py:158
  112.7 37.5 %all-to-all-start.7 = ((f32[2,128,1024]{2,0,1:T(2,128)}), f32[2,128,1024]{2,0,1:T(2,128)}, u32[]{:S(2)}, u32[]{:S(2)}) async-start(f32[2,128,1024]{2,0,1:T(2,128)} %pad_maximum_fusion.2), calls=%async_computation.7 | async-start | bytes 2097152 | tf_op jit(solution)/shard_map/all_to_all | solution.py:165
  132.0 36.0 %copy-start.1 = (f32[2,32,32,64]{3,2,1,0:T(8,128)}, f32[2,32,32,64]{3,2,1,0:T(8,128)S(1)}, u32[]{:S(2)}) copy-start(f32[2,32,32,64]{3,2,1,0:T(8,128)S(1)} %reshape.614) | copy-start | bytes 1572868
  138.2 32.4 %copy-start.2 = (f32[2,32,32,64]{3,2,1,0:T(8,128)}, f32[2,32,32,64]{3,2,1,0:T(8,128)S(1)}, u32[]{:S(2)}) copy-start(f32[2,32,32,64]{3,2,1,0:T(8,128)S(1)} %reshape.617) | copy-start | bytes 1572868
  236.3 47.6 %copy-start.5 = (f32[1,2,65536]{2,1,0:T(2,128)S(1)}, f32[1,2,65536]{2,1,0:T(2,128)}, u32[]{:S(2)}) copy-start(f32[1,2,65536]{2,1,0:T(2,128)} %get-tuple-element.40) | copy-start | bytes 1572868
  236.4 47.6 %copy-start.6 = (f32[1,2,65536]{2,1,0:T(2,128)S(1)}, f32[1,2,65536]{2,1,0:T(2,128)}, u32[]{:S(2)}) copy-start(f32[1,2,65536]{2,1,0:T(2,128)} %get-tuple-element.41) | copy-start | bytes 1572868
  275.2 163.8 %all-to-all-start.4 = ((f32[64,2,2,1024]{3,2,1,0:T(2,128)}), f32[64,2,2,1024]{3,2,1,0:T(2,128)S(1)}, u32[]{:S(2)}, u32[]{:S(2)}) async-start(f32[64,2,2,1024]{3,2,1,0:T(2,128)} %constant_dynamic-update-slice_fusion), calls=%async_computation.4 | async-start | bytes 2097152 | tf_op jit(solution)/shard_map/all_to_all | solution.py:13
  439.0 167.8 %all-to-all-start.8 = ((f32[64,1,4096]{2,1,0:T(1,128)}), f32[64,1,4096]{2,1,0:T(1,128)S(1)}, u32[]{:S(2)}, u32[]{:S(2)}) async-start(f32[64,1,4096]{2,1,0:T(1,128)} %reshape.651), calls=%async_computation.8 | async-start | bytes 2097152 | tf_op jit(solution)/shard_map/all_to_all | solution.py:185
  606.8 218.7 %all-to-all-start.10 = ((f32[64,1,4096]{2,1,0:T(1,128)}), f32[64,1,4096]{2,1,0:T(1,128)S(1)}, u32[]{:S(2)}, u32[]{:S(2)}) async-start(f32[64,1,4096]{2,1,0:T(1,128)} %reshape.655), calls=%async_computation.10 | async-start | bytes 2097152 | tf_op jit(solution)/shard_map/all_to_all | solution.py:188
  825.6 214.0 %all-to-all-start.5 = ((bf16[64,2,512]{2,1,0:T(2,128)(2,1)}), bf16[64,2,512]{2,1,0:T(2,128)(2,1)S(1)}, u32[]{:S(2)}, u32[]{:S(2)}) async-start(bf16[64,2,512]{2,1,0:T(2,128)(2,1)} %reshape.647), calls=%async_computation.5 | async-start | bytes 262144 | tf_op jit(solution)/shard_map/all_to_all | solution.py:196
  838.0 233.4 %copy-start.4 = (f32[1024,64]{0,1:T(8,128)S(1)}, f32[1024,64]{0,1:T(8,128)}, u32[]{:S(2)}) copy-start(f32[1024,64]{0,1:T(8,128)} %copy-done.3) | copy-start | bytes 786436
  838.0 233.4 %copy-start.13 = (f32[1024]{0:T(1024)S(1)}, f32[1024]{0:T(1024)}, u32[]{:S(2)}) copy-start(f32[1024]{0:T(1024)} %copy-done.12) | copy-start | bytes 12292
  838.0 233.4 %copy-start.15 = (f32[64]{0:T(128)S(1)}, f32[64]{0:T(128)}, u32[]{:S(2)}) copy-start(f32[64]{0:T(128)} %copy-done.14) | copy-start | bytes 772
  838.1 233.4 %copy-start.17 = (f32[64]{0:T(128)S(1)}, f32[64]{0:T(128)}, u32[]{:S(2)}) copy-start(f32[64]{0:T(128)} %copy-done.16) | copy-start | bytes 772
  838.1 233.9 %copy-start.7 = (f32[1024,64]{0,1:T(8,128)S(1)}, f32[1024,64]{0,1:T(8,128)}, u32[]{:S(2)}) copy-start(f32[1024,64]{0,1:T(8,128)} %get-tuple-element.71) | copy-start | bytes 786436
  838.1 235.2 %copy-start.9 = (f32[1024,16]{0,1:T(8,128)S(1)}, f32[1024,16]{0,1:T(8,128)}, u32[]{:S(2)}) copy-start(f32[1024,16]{0,1:T(8,128)} %copy-done.8) | copy-start | bytes 196612
  838.1 235.2 %copy-start.11 = (f32[1024,16]{0,1:T(8,128)S(1)}, f32[1024,16]{0,1:T(8,128)}, u32[]{:S(2)}) copy-start(f32[1024,16]{0,1:T(8,128)} %copy-done.10) | copy-start | bytes 196612
  1039.6 17.5 %all-to-all-start.9 = ((bf16[64,2,512]{2,1,0:T(2,128)(2,1)}), bf16[64,2,512]{2,1,0:T(2,128)(2,1)S(1)}, u32[]{:S(2)}, u32[]{:S(2)}) async-start(bf16[64,2,512]{2,1,0:T(2,128)(2,1)} %reshape.653), calls=%async_computation.9 | async-start | bytes 262144 | tf_op jit(solution)/shard_map/all_to_all | solution.py:203
  1057.1 13.2 all-to-all-start.11
